TPU v7x, 512 devices: a whole 4x4x16 slice. The times are simulated.
512 devices in a mesh: tgt: 16 (over z), src: 32 (over x, y, core).
Axes of the slice: x: 4, y: 4, z: 16, core: 2. Of those that a mesh axis runs over, the one named last changes fastest.
Arguments:
- target_xy: float32 [2, 8192], P(None, 'tgt'), may hold values from 0 to 20
- source_xy: float32 [2, 65536], P(None, 'src'), may hold values from 0 to 20
- body_of: int32 [65536], P('src'), may hold values from 0 to 127
- series_coef: float32 [2, 32, 128], replicated, may hold values from -2 to 2
- probe_matrix: bfloat16 [65536, 128], P('src'), may hold values from -0.0234375 to 0.0234375
- row_weight: float32 [8192], P('tgt'), may hold values from 1 to 36
Outputs:
- basis: float32 [8192, 256], P(('tgt', 'src'))
- factor: float32 [128, 128], replicated
All inputs are finite; a program needn't handle non-finite values.
Results may differ from a plain program's by a relative error of at most 0.0085.
Values sent between devices are 32-bit elements; how exact they have to be, the bound alone decides.
No kernel may reach another device: no remote copies, remote signals or barrier semaphores. Data moves between devices by JAX's collectives and lax.ppermute only.
A program may use at most 64 MiB of HBM per device.

v0:
```python
import math

import jax
import jax.numpy as jnp
from jax import lax
from jax.experimental import pallas as pl
from jax.experimental.pallas import tpu as pltpu
from jax.sharding import PartitionSpec as P

NTERMS = 32
SUB_ROWS = 32
LANES = 128
COL_BLOCK = 512


def sketch_kernel(txy_ref, sxy_ref, coef_ref, probe_ref, out_ref, re_scr, im_scr):
    col_step = pl.program_id(0)
    rows = re_scr.shape[0]
    groups = re_scr.shape[1] // LANES
    terms = coef_ref.shape[0] // 2

    @pl.when(col_step == 0)
    def _():
        out_ref[...] = jnp.zeros_like(out_ref)

    def one_sub(index, carry):
        row_at = pl.multiple_of((index // groups) * SUB_ROWS, SUB_ROWS)
        col_at = pl.multiple_of((index % groups) * LANES, LANES)
        tx = txy_ref[0, pl.ds(row_at, SUB_ROWS), :]
        ty = txy_ref[1, pl.ds(row_at, SUB_ROWS), :]
        sx = sxy_ref[pl.ds(0, 1), pl.ds(col_at, LANES)]
        sy = sxy_ref[pl.ds(1, 1), pl.ds(col_at, LANES)]
        delta_x = tx - sx
        delta_y = ty - sy
        radius = jnp.sqrt(delta_x * delta_x + delta_y * delta_y + 0.25)
        decay_rate = jnp.exp(-0.005 * radius)
        step_re = decay_rate * jnp.cos(1.5 * radius)
        step_im = decay_rate * jnp.sin(1.5 * radius)

        def coef(n):
            return (coef_ref[pl.ds(n, 1), pl.ds(col_at, LANES)],
                    coef_ref[pl.ds(terms + n, 1), pl.ds(col_at, LANES)])

        last_re, last_im = coef(terms - 1)
        total_re = jnp.broadcast_to(last_re, radius.shape)
        total_im = jnp.broadcast_to(last_im, radius.shape)
        for degree in range(terms - 2, -1, -1):
            c_re, c_im = coef(degree)
            next_re = total_re * step_re - total_im * step_im + c_re
            next_im = total_re * step_im + total_im * step_re + c_im
            total_re, total_im = next_re, next_im
        series_re = total_re * step_re - total_im * step_im
        series_im = total_re * step_im + total_im * step_re
        re_scr[pl.ds(row_at, SUB_ROWS), pl.ds(col_at, LANES)] = (1.0 / radius + series_re).astype(jnp.bfloat16)
        im_scr[pl.ds(row_at, SUB_ROWS), pl.ds(col_at, LANES)] = series_im.astype(jnp.bfloat16)
        return carry

    lax.fori_loop(0, (rows // SUB_ROWS) * groups, one_sub, 0)
    probe = probe_ref[...]
    rank = probe.shape[1]
    out_ref[:, :rank] += jnp.dot(re_scr[...], probe, preferred_element_type=jnp.float32)
    out_ref[:, rank:] += jnp.dot(im_scr[...], probe, preferred_element_type=jnp.float32)


def sketch_pallas(target_xy, source_xy, picked, probe_matrix):
    rows = target_xy.shape[1]
    sources = source_xy.shape[1]
    rank = probe_matrix.shape[1]
    col_block = min(COL_BLOCK, sources)
    txy = jnp.broadcast_to(target_xy[:, :, None], (2, rows, LANES))
    return pl.pallas_call(
        sketch_kernel,
        grid=(sources // col_block,),
        in_specs=[
            pl.BlockSpec((2, rows, LANES), lambda j: (0, 0, 0)),
            pl.BlockSpec((2, col_block), lambda j: (0, j)),
            pl.BlockSpec((picked.shape[0], col_block), lambda j: (0, j)),
            pl.BlockSpec((col_block, rank), lambda j: (j, 0)),
        ],
        out_specs=pl.BlockSpec((rows, 2 * rank), lambda j: (0, 0)),
        out_shape=jax.ShapeDtypeStruct((rows, 2 * rank), jnp.float32),
        scratch_shapes=[pltpu.VMEM((rows, col_block), jnp.bfloat16),
                        pltpu.VMEM((rows, col_block), jnp.bfloat16)],
    )(txy, source_xy, picked, probe_matrix)


def in_blocks(array, dim, count):
    shape = array.shape
    tiles = array.reshape(*shape[:dim], count, shape[dim] // count, *shape[dim + 1 :])
    return jnp.moveaxis(tiles, dim, 0)


def sent_and_summed(array, axis, dim):
    tiles = in_blocks(array, dim, lax.axis_size(axis))
    arrived = lax.all_to_all(tiles, axis, split_axis=0, concat_axis=0, tiled=True)
    return arrived.sum(axis=0)


def from_everyone(array, axis):
    copies = jnp.broadcast_to(array, (lax.axis_size(axis), *array.shape))
    return lax.all_to_all(copies, axis, split_axis=0, concat_axis=0, tiled=True)


def of_everyone(array, axis):
    everything = from_everyone(array, axis)
    return jnp.sum(everything, axis=0)


def panel_series(rows_xy, cols_xy, coef_re, coef_im):
    delta_x = rows_xy[0][:, None] - cols_xy[0][None, :]
    delta_y = rows_xy[1][:, None] - cols_xy[1][None, :]
    radius = jnp.sqrt(delta_x * delta_x + delta_y * delta_y + 0.25)
    decay_rate = jnp.exp(-0.005 * radius)
    step_re = decay_rate * jnp.cos(1.5 * radius)
    step_im = decay_rate * jnp.sin(1.5 * radius)
    term_count = coef_re.shape[0]
    total_re = jnp.broadcast_to(coef_re[term_count - 1][None, :], radius.shape)
    total_im = jnp.broadcast_to(coef_im[term_count - 1][None, :], radius.shape)
    for degree in range(term_count - 2, -1, -1):
        next_re = total_re * step_re - total_im * step_im + coef_re[degree][None, :]
        next_im = total_re * step_im + total_im * step_re + coef_im[degree][None, :]
        total_re, total_im = (next_re, next_im)
    series_re = total_re * step_re - total_im * step_im
    series_im = total_re * step_im + total_im * step_re
    tile_re = (1.0 / radius + series_re).astype(jnp.bfloat16)
    tile_im = series_im.astype(jnp.bfloat16)
    return (tile_re, tile_im)


def sketch_rows(target_xy, source_xy, picked, probe_matrix, row_count):
    source_count = probe_matrix.shape[0]
    block_width = math.gcd(source_count, 1024)
    blocks = source_count // block_width
    rank_width = probe_matrix.shape[1]

    def add_block(block_index, totals):
        block_start = block_index * block_width
        xy_block = lax.dynamic_slice_in_dim(source_xy, block_start, block_width, 1)
        coef_block = lax.dynamic_slice_in_dim(picked, block_start, block_width, 1)
        probe_block = lax.dynamic_slice_in_dim(probe_matrix, block_start, block_width, 0)
        tile_re, tile_im = panel_series(
            target_xy, xy_block, coef_block[:NTERMS], coef_block[NTERMS:]
        )
        part_re = jnp.dot(tile_re, probe_block, preferred_element_type=jnp.float32)
        part_im = jnp.dot(tile_im, probe_block, preferred_element_type=jnp.float32)
        return totals + jnp.concatenate([part_re, part_im], axis=1)

    start_totals = jnp.zeros((row_count, 2 * rank_width), jnp.float32)
    return lax.fori_loop(0, blocks, add_block, start_totals)


def gram_of(rows_part, scale_rows):
    rank_width = rows_part.shape[1] // 2
    stacked = rows_part.reshape(-1, rank_width)
    return jnp.dot(stacked.T, stacked, precision=lax.Precision.HIGHEST) / scale_rows


def pick_coefficients(series_coef, body_of):
    bodies = series_coef.shape[2]
    one_hot = (jnp.arange(bodies, dtype=jnp.int32)[:, None] == body_of[None, :]).astype(
        jnp.bfloat16
    )
    table = series_coef.reshape(-1, bodies)
    high_part = table.astype(jnp.bfloat16)
    rest_one = table - high_part.astype(jnp.float32)
    middle_part = rest_one.astype(jnp.bfloat16)
    low_part = (rest_one - middle_part.astype(jnp.float32)).astype(jnp.bfloat16)
    picked = jnp.dot(high_part, one_hot, preferred_element_type=jnp.float32)
    picked = picked + jnp.dot(middle_part, one_hot, preferred_element_type=jnp.float32)
    return picked + jnp.dot(low_part, one_hot, preferred_element_type=jnp.float32)


def per_device(target_xy, source_xy, body_of, series_coef, probe_matrix, row_weight):
    rank_width = probe_matrix.shape[1]
    picked = pick_coefficients(series_coef, body_of)
    rows_all = target_xy.shape[1]
    own_count = rows_all // lax.axis_size("src")
    scale_rows = float(2 * rows_all * lax.axis_size("tgt"))
    own_start = lax.axis_index("src") * own_count
    own_sum = sent_and_summed(
        sketch_pallas(target_xy, source_xy, picked, probe_matrix),
        "src",
        0,
    )
    own_weight = lax.dynamic_slice_in_dim(row_weight, own_start, own_count, 0)
    own_rows = own_sum * own_weight[:, None]
    local_gram = gram_of(own_rows, scale_rows)
    gram_piece = sent_and_summed(local_gram, "src", 0)
    gram_piece = of_everyone(gram_piece, "tgt")
    full_gram = from_everyone(gram_piece, "src").reshape(rank_width, rank_width)
    lower_factor = jnp.linalg.cholesky(full_gram)
    identity = jnp.eye(rank_width, dtype=jnp.float32)
    inverse = lax.linalg.triangular_solve(lower_factor, identity, left_side=True, lower=True)
    basis_rows = jnp.dot(
        own_rows.reshape(-1, rank_width), inverse.T, precision=lax.Precision.HIGHEST
    )
    return (basis_rows.reshape(own_count, 2 * rank_width), lower_factor.T)


def solution(mesh):
    return jax.shard_map(
        per_device,
        mesh=mesh,
        in_specs=(P(None, "tgt"), P(None, "src"), P("src"), P(), P("src", None), P("tgt")),
        out_specs=(P(("tgt", "src"), None), P()),
        check_vma=False,
    )
```

profile of v0, /device:TPU:1, one launch (start us, length us, event | category | flops | bytes accessed | tf_op | source)
XLA Modules:
  0.0 173.3 jit_solution(12305101247754016917)
XLA Ops:
  0.6 0.0 copy-start
  0.6 0.8 bitcast_convert_fusion
  1.5 0.0 copy-done
  1.5 0.7 copy-done.1
  2.2 0.3 convolution_bitcast_fusion
  2.5 0.3 convolution_add_fusion.1
  2.8 0.0 copy-start.2
  2.8 1.1 convolution_add_fusion.coef_ref
  4.0 0.0 copy-done.2
  4.0 1.0 broadcast_in_dim.7.txy_ref
  4.9 72.4 %shard_map.77 = f32[512,256]{1,0:T(8,128)} custom-call(f32[2,512,128]{2,1,0:T(8,128)} %broadcast_in_dim.7.txy_ref, f32[2,2048]{1,0:T(2,128)} %sxy_ref.1, f32[64,2048]{1,0:T(8,128)} %convolution_add_fusion.coef_ref, bf16[2048,128]{1,0:T(8,128)(2,1)} %probe_ref.1), custom_call_target="tpu_custom_call" | custom-call | tf_op jit(solution)/shard_map/pallas_call | solution.py:71
  77.4 10.4 %all-to-all-start = ((f32[32,16,256]{2,1,0:T(8,128)}), f32[32,16,256]{2,1,0:T(8,128)S(1)}, u32[]{:S(2)}, u32[]{:S(2)}) async-start(f32[32,16,256]{2,1,0:T(8,128)} %bitcast.35), calls=%async_computation | async-start | bytes 1048576 | tf_op jit(solution)/shard_map/all_to_all | solution.py:95
  87.7 0.8 dynamic_slice.3
  88.5 10.9 %all-to-all-done = f32[32,16,256]{2,1,0:T(8,128)S(1)} async-done(((f32[32,16,256]{2,1,0:T(8,128)}), f32[32,16,256]{2,1,0:T(8,128)S(1)}, u32[]{:S(2)}, u32[]{:S(2)}) %all-to-all-start) | async-done | bytes 524320 | tf_op jit(solution)/shard_map/all_to_all | solution.py:95
  99.5 0.1 broadcast_multiply_fusion
  99.6 0.3 convolution_multiply_fusion
  99.9 10.8 %all_to_all.20 = f32[32,4,128]{2,1,0:T(4,128)S(1)} all-to-all(f32[32,4,128]{2,1,0:T(4,128)S(1)} %bitcast.38), channel_id=1, replica_groups=mesh['tgt'=16,'src'=32] {'src'}, dimensions={0} | all-to-all | bytes 131072 | tf_op jit(solution)/shard_map/all_to_all | solution.py:95
  110.7 24.3 %all_to_all.21 = f32[16,4,128]{2,1,0:T(4,128)S(1)} all-to-all(f32[16,4,128]{2,1,0:T(4,128)S(1)} %broadcast_in_dim.8), channel_id=1, replica_groups=mesh['tgt'=16,'src'=32] {'tgt'}, dimensions={0} | all-to-all | bytes 65536 | tf_op jit(solution)/shard_map/all_to_all | solution.py:101
  135.0 0.6 broadcast_in_dim.9
  135.7 5.3 %all-to-all-start.3 = ((f32[32,4,128]{2,1,0:T(4,128)}), f32[32,4,128]{2,1,0:T(4,128)S(1)}, u32[]{:S(2)}, u32[]{:S(2)}) async-start(f32[32,4,128]{2,1,0:T(4,128)} %broadcast_in_dim.9), calls=%async_computation.3 | async-start | bytes 131072 | tf_op jit(solution)/shard_map/all_to_all | solution.py:101
  140.9 0.1 mul.34
  141.0 0.1 mul.35
  141.1 7.3 %all-to-all-done.3 = f32[32,4,128]{2,1,0:T(4,128)S(1)} async-done(((f32[32,4,128]{2,1,0:T(4,128)}), f32[32,4,128]{2,1,0:T(4,128)S(1)}, u32[]{:S(2)}, u32[]{:S(2)}) %all-to-all-start.3) | async-done | bytes 65568 | tf_op jit(solution)/shard_map/all_to_all | solution.py:101
  148.4 0.1 copy.15
  148.5 11.7 %cholesky.17 = f32[128,128]{1,0:T(8,128)S(1)} custom-call(f32[128,128]{1,0:T(8,128)S(1)} %fusion.5), custom_call_target="Cholesky" | custom-call | tf_op jit(solution)/shard_map/jit(cholesky)/cholesky | solution.py:191
  160.3 0.6 compare_reduce_fusion
  160.9 0.7 fusion.6
  161.6 9.8 %custom-call.6 = f32[1,128,128]{1,2,0:T(8,128)S(1)} custom-call(f32[1,128,128]{2,1,0:T(8,128)S(1)} %get-tuple-element.11), custom_call_target="InvertDiagBlocksLowerTriangular" | custom-call | tf_op jit(solution)/shard_map/triangular_solve | solution.py:193
  171.4 0.2 fusion.3
  171.6 0.2 fusion.8
  171.9 0.6 reshape.77
  172.5 0.7 copy.16
  (10 shorter events, 0.2 us)
Async XLA Ops:
  0.6 0.8 copy-start
  1.5 0.7 copy-start.1
  2.8 1.1 copy-start.2
  77.4 22.1 %all-to-all-start = ((f32[32,16,256]{2,1,0:T(8,128)}), f32[32,16,256]{2,1,0:T(8,128)S(1)}, u32[]{:S(2)}, u32[]{:S(2)}) async-start(f32[32,16,256]{2,1,0:T(8,128)} %bitcast.35), calls=%async_computation | async-start | bytes 1048576 | tf_op jit(solution)/shard_map/all_to_all | solution.py:95
  135.7 12.7 %all-to-all-start.3 = ((f32[32,4,128]{2,1,0:T(4,128)}), f32[32,4,128]{2,1,0:T(4,128)S(1)}, u32[]{:S(2)}, u32[]{:S(2)}) async-start(f32[32,4,128]{2,1,0:T(4,128)} %broadcast_in_dim.9), calls=%async_computation.3 | async-start | bytes 131072 | tf_op jit(solution)/shard_map/all_to_all | solution.py:101
where the time goes:
time: 174 us; the launch traced here: 173 us
  Pallas kernels  72.4 us (42%)
  blocking collectives  35.1 us (20%)
  other arithmetic  23.9 us (14%)
  waiting for transfers between devices  18.2 us (10%)
  starting transfers between devices  15.6 us (9%)
  local copies, waits for them, and re-layouts  4.72 us (3%)
  matrix products  2.54 us (1%)
    pallas_call x1, Pallas kernels, sketch_pallas(): pl.pallas_call(sketch_kernel, grid=(sources // col_block,), in_specs=[pl....  72.4 us
    all_to_all x1, blocking collectives, from_everyone(): return lax.all_to_all(copies, axis, split_axis=0, concat_axis=0, tiled=True)  24.3 us
    another operation x3, other arithmetic, per_device(): lower_factor = jnp.linalg.cholesky(full_gram)  12.4 us
    all_to_all x1, waiting for transfers between devices, sent_and_summed(): lax.all_to_all(tiles, axis, split_axis=0, concat_axis=0, tiled=True)  10.9 us
    all_to_all x1, blocking collectives, sent_and_summed(): lax.all_to_all(tiles, axis, split_axis=0, concat_axis=0, tiled=True)  10.8 us
    all_to_all x1, starting transfers between devices, sent_and_summed(): lax.all_to_all(tiles, axis, split_axis=0, concat_axis=0, tiled=True)  10.4 us
    another operation x1, other arithmetic, per_device(): lax.linalg.triangular_solve(lower_factor, identity, left_side=True, lower...  9.81 us
    all_to_all x1, waiting for transfers between devices, from_everyone(): return lax.all_to_all(copies, axis, split_axis=0, concat_axis=0, tiled=True)  7.3 us
  transfers between devices with their start and end apart: 2, of which 2 were waited for; matrix products, arithmetic and copies ran while one was open for 1% of the time, Pallas kernels for 0%

commit v1 on v0

--- a/solution.py
+++ b/solution.py
@@ -8,9 +8,30 @@
 from jax.sharding import PartitionSpec as P
 
 NTERMS = 32
-SUB_ROWS = 32
+SUB_ROWS = 64
 LANES = 128
 COL_BLOCK = 512
+
+
+def cos_and_sin(angle):
+    quarter = jnp.floor(angle * 0.6366197723675814 + 0.5)
+    rest = angle - quarter * 1.5703125
+    rest = rest - quarter * 4.837512969970703125e-4
+    rest = rest - quarter * 7.54978995489188216e-8
+    square = rest * rest
+    sin_rest = rest + rest * square * (
+        -1.6666654611e-1 + square * (8.3321608736e-3 + square * -1.9515295891e-4)
+    )
+    cos_rest = (1.0 - 0.5 * square) + square * square * (
+        4.166664568298827e-2 + square * (-1.388731625493765e-3 + square * 2.443315711809948e-5)
+    )
+    turn = quarter.astype(jnp.int32)
+    swap = (turn & 1) == 1
+    sin_value = jnp.where(swap, cos_rest, sin_rest)
+    cos_value = jnp.where(swap, sin_rest, cos_rest)
+    sin_value = jnp.where((turn & 2) == 2, -sin_value, sin_value)
+    cos_value = jnp.where(((turn + 1) & 2) == 2, -cos_value, cos_value)
+    return cos_value, sin_value
 
 
 def sketch_kernel(txy_ref, sxy_ref, coef_ref, probe_ref, out_ref, re_scr, im_scr):
@@ -34,8 +55,9 @@
         delta_y = ty - sy
         radius = jnp.sqrt(delta_x * delta_x + delta_y * delta_y + 0.25)
         decay_rate = jnp.exp(-0.005 * radius)
-        step_re = decay_rate * jnp.cos(1.5 * radius)
-        step_im = decay_rate * jnp.sin(1.5 * radius)
+        cos_part, sin_part = cos_and_sin(1.5 * radius)
+        step_re = decay_rate * cos_part
+        step_im = decay_rate * sin_part
 
         def coef(n):
             return (coef_ref[pl.ds(n, 1), pl.ds(col_at, LANES)],
@@ -55,7 +77,7 @@
         im_scr[pl.ds(row_at, SUB_ROWS), pl.ds(col_at, LANES)] = series_im.astype(jnp.bfloat16)
         return carry
 
-    lax.fori_loop(0, (rows // SUB_ROWS) * groups, one_sub, 0)
+    lax.fori_loop(0, (rows // SUB_ROWS) * groups, one_sub, 0, unroll=2)
     probe = probe_ref[...]
     rank = probe.shape[1]
     out_ref[:, :rank] += jnp.dot(re_scr[...], probe, preferred_element_type=jnp.float32)

time: 174 us -> 153 us (0.88)
  Pallas kernels: 72.4 us -> 51.4 us
    pallas_call x1, Pallas kernels: 72.4 us -> 51.4 us  [sketch_pallas(): pl.pallas_call(sketch_kernel, grid=(sources // col_block,), in_specs=[pl....]
where the time goes in v1:
time: 153 us; the launch traced here: 152 us
  Pallas kernels  51.4 us (34%)
  blocking collectives  35.1 us (23%)
  other arithmetic  23.9 us (16%)
  waiting for transfers between devices  18.2 us (12%)
  starting transfers between devices  15.6 us (10%)
  local copies, waits for them, and re-layouts  4.72 us (3%)
  matrix products  2.54 us (2%)
    pallas_call x1, Pallas kernels, sketch_pallas(): pl.pallas_call(sketch_kernel, grid=(sources // col_block,), in_specs=[pl....  51.4 us
    all_to_all x1, blocking collectives, from_everyone(): return lax.all_to_all(copies, axis, split_axis=0, concat_axis=0, tiled=True)  24.3 us
    another operation x3, other arithmetic, per_device(): lower_factor = jnp.linalg.cholesky(full_gram)  12.4 us
    all_to_all x1, waiting for transfers between devices, sent_and_summed(): lax.all_to_all(tiles, axis, split_axis=0, concat_axis=0, tiled=True)  10.9 us
    all_to_all x1, blocking collectives, sent_and_summed(): lax.all_to_all(tiles, axis, split_axis=0, concat_axis=0, tiled=True)  10.8 us
    all_to_all x1, starting transfers between devices, sent_and_summed(): lax.all_to_all(tiles, axis, split_axis=0, concat_axis=0, tiled=True)  10.4 us
    another operation x1, other arithmetic, per_device(): lax.linalg.triangular_solve(lower_factor, identity, left_side=True, lower...  9.81 us
    all_to_all x1, waiting for transfers between devices, from_everyone(): return lax.all_to_all(copies, axis, split_axis=0, concat_axis=0, tiled=True)  7.3 us
  transfers between devices with their start and end apart: 2, of which 2 were waited for; matrix products, arithmetic and copies ran while one was open for 1% of the time, Pallas kernels for 0%

profile of v1, /device:TPU:1, one launch (start us, length us, event | category | flops | bytes accessed | tf_op | source)
XLA Modules:
  0.0 152.2 jit_solution(9200847673339606707)
XLA Ops:
  0.6 0.0 copy-start
  0.6 0.8 bitcast_convert_fusion
  1.5 0.0 copy-done
  1.5 0.7 copy-done.1
  2.2 0.3 convolution_bitcast_fusion
  2.5 0.3 convolution_add_fusion.1
  2.8 0.0 copy-start.2
  2.8 1.1 convolution_add_fusion.coef_ref
  4.0 0.0 copy-done.2
  4.0 1.0 broadcast_in_dim.7.txy_ref
  4.9 51.4 %shard_map.77 = f32[512,256]{1,0:T(8,128)} custom-call(f32[2,512,128]{2,1,0:T(8,128)} %broadcast_in_dim.7.txy_ref, f32[2,2048]{1,0:T(2,128)} %sxy_ref.1, f32[64,2048]{1,0:T(8,128)} %convolution_add_fusion.coef_ref, bf16[2048,128]{1,0:T(8,128)(2,1)} %probe_ref.1), custom_call_target="tpu_custom_call" | custom-call | tf_op jit(solution)/shard_map/pallas_call | solution.py:93
  56.3 10.4 %all-to-all-start = ((f32[32,16,256]{2,1,0:T(8,128)}), f32[32,16,256]{2,1,0:T(8,128)S(1)}, u32[]{:S(2)}, u32[]{:S(2)}) async-start(f32[32,16,256]{2,1,0:T(8,128)} %bitcast.35), calls=%async_computation | async-start | bytes 1048576 | tf_op jit(solution)/shard_map/all_to_all | solution.py:117
  66.7 0.8 dynamic_slice.3
  67.5 10.9 %all-to-all-done = f32[32,16,256]{2,1,0:T(8,128)S(1)} async-done(((f32[32,16,256]{2,1,0:T(8,128)}), f32[32,16,256]{2,1,0:T(8,128)S(1)}, u32[]{:S(2)}, u32[]{:S(2)}) %all-to-all-start) | async-done | bytes 524320 | tf_op jit(solution)/shard_map/all_to_all | solution.py:117
  78.5 0.1 broadcast_multiply_fusion
  78.5 0.3 convolution_multiply_fusion
  78.8 10.8 %all_to_all.20 = f32[32,4,128]{2,1,0:T(4,128)S(1)} all-to-all(f32[32,4,128]{2,1,0:T(4,128)S(1)} %bitcast.38), channel_id=1, replica_groups=mesh['tgt'=16,'src'=32] {'src'}, dimensions={0} | all-to-all | bytes 131072 | tf_op jit(solution)/shard_map/all_to_all | solution.py:117
  89.6 24.3 %all_to_all.21 = f32[16,4,128]{2,1,0:T(4,128)S(1)} all-to-all(f32[16,4,128]{2,1,0:T(4,128)S(1)} %broadcast_in_dim.8), channel_id=1, replica_groups=mesh['tgt'=16,'src'=32] {'tgt'}, dimensions={0} | all-to-all | bytes 65536 | tf_op jit(solution)/shard_map/all_to_all | solution.py:123
  114.0 0.6 broadcast_in_dim.9
  114.6 5.3 %all-to-all-start.3 = ((f32[32,4,128]{2,1,0:T(4,128)}), f32[32,4,128]{2,1,0:T(4,128)S(1)}, u32[]{:S(2)}, u32[]{:S(2)}) async-start(f32[32,4,128]{2,1,0:T(4,128)} %broadcast_in_dim.9), calls=%async_computation.3 | async-start | bytes 131072 | tf_op jit(solution)/shard_map/all_to_all | solution.py:123
  119.9 0.1 mul.34
  120.0 0.1 mul.35
  120.1 7.3 %all-to-all-done.3 = f32[32,4,128]{2,1,0:T(4,128)S(1)} async-done(((f32[32,4,128]{2,1,0:T(4,128)}), f32[32,4,128]{2,1,0:T(4,128)S(1)}, u32[]{:S(2)}, u32[]{:S(2)}) %all-to-all-start.3) | async-done | bytes 65568 | tf_op jit(solution)/shard_map/all_to_all | solution.py:123
  127.4 0.1 copy.15
  127.5 11.7 %cholesky.17 = f32[128,128]{1,0:T(8,128)S(1)} custom-call(f32[128,128]{1,0:T(8,128)S(1)} %fusion.5), custom_call_target="Cholesky" | custom-call | tf_op jit(solution)/shard_map/jit(cholesky)/cholesky | solution.py:213
  139.2 0.6 compare_reduce_fusion
  139.9 0.7 fusion.6
  140.5 9.8 %custom-call.6 = f32[1,128,128]{1,2,0:T(8,128)S(1)} custom-call(f32[1,128,128]{2,1,0:T(8,128)S(1)} %get-tuple-element.11), custom_call_target="InvertDiagBlocksLowerTriangular" | custom-call | tf_op jit(solution)/shard_map/triangular_solve | solution.py:215
  150.3 0.2 fusion.3
  150.6 0.2 fusion.8
  150.8 0.6 reshape.77
  151.5 0.7 copy.16
  (10 shorter events, 0.2 us)
Async XLA Ops:
  0.6 0.8 copy-start
  1.5 0.7 copy-start.1
  2.8 1.1 copy-start.2
  56.3 22.1 %all-to-all-start = ((f32[32,16,256]{2,1,0:T(8,128)}), f32[32,16,256]{2,1,0:T(8,128)S(1)}, u32[]{:S(2)}, u32[]{:S(2)}) async-start(f32[32,16,256]{2,1,0:T(8,128)} %bitcast.35), calls=%async_computation | async-start | bytes 1048576 | tf_op jit(solution)/shard_map/all_to_all | solution.py:117
  114.6 12.7 %all-to-all-start.3 = ((f32[32,4,128]{2,1,0:T(4,128)}), f32[32,4,128]{2,1,0:T(4,128)S(1)}, u32[]{:S(2)}, u32[]{:S(2)}) async-start(f32[32,4,128]{2,1,0:T(4,128)} %broadcast_in_dim.9), calls=%async_computation.3 | async-start | bytes 131072 | tf_op jit(solution)/shard_map/all_to_all | solution.py:123

commit v2 on v1

--- a/solution.py
+++ b/solution.py
@@ -106,6 +106,44 @@
     )(txy, source_xy, picked, probe_matrix)
 
 
+def factor_kernel(gram_ref, upper_ref, inverse_ref):
+    size = gram_ref.shape[0]
+    upper_ref[...] = gram_ref[...]
+    rows = lax.broadcasted_iota(jnp.int32, (size, size), 0)
+    cols = lax.broadcasted_iota(jnp.int32, (size, size), 1)
+    inverse_ref[...] = jnp.where(rows == cols, 1.0, 0.0).astype(jnp.float32)
+    lane = lax.broadcasted_iota(jnp.int32, (1, size), 1)
+    sublane = lax.broadcasted_iota(jnp.int32, (size, 1), 0)
+
+    def step(j, carry):
+        left = upper_ref[...]
+        row_left = upper_ref[pl.ds(j, 1), :]
+        row_right = inverse_ref[pl.ds(j, 1), :]
+        pivot = jnp.sum(jnp.where(lane == j, row_left, 0.0), axis=1, keepdims=True)
+        scale = 1.0 / jnp.sqrt(pivot)
+        pivot_left = jnp.where(lane >= j, row_left * scale, 0.0)
+        pivot_right = row_right * scale
+        column = jnp.sum(jnp.where(cols == j, left, 0.0), axis=1, keepdims=True)
+        multiplier = jnp.where(sublane > j, column * scale, 0.0)
+        upper_ref[...] = left - multiplier * pivot_left
+        inverse_ref[...] = inverse_ref[...] - multiplier * pivot_right
+        upper_ref[pl.ds(j, 1), :] = pivot_left
+        inverse_ref[pl.ds(j, 1), :] = pivot_right
+        return carry
+
+    lax.fori_loop(0, size, step, 0)
+    upper_ref[...] = jnp.where(rows <= cols, upper_ref[...], 0.0)
+
+
+def factor_pallas(gram):
+    size = gram.shape[0]
+    return pl.pallas_call(
+        factor_kernel,
+        out_shape=(jax.ShapeDtypeStruct((size, size), jnp.float32),
+                   jax.ShapeDtypeStruct((size, size), jnp.float32)),
+    )(gram)
+
+
 def in_blocks(array, dim, count):
     shape = array.shape
     tiles = array.reshape(*shape[:dim], count, shape[dim] // count, *shape[dim + 1 :])
@@ -210,13 +248,11 @@
     gram_piece = sent_and_summed(local_gram, "src", 0)
     gram_piece = of_everyone(gram_piece, "tgt")
     full_gram = from_everyone(gram_piece, "src").reshape(rank_width, rank_width)
-    lower_factor = jnp.linalg.cholesky(full_gram)
-    identity = jnp.eye(rank_width, dtype=jnp.float32)
-    inverse = lax.linalg.triangular_solve(lower_factor, identity, left_side=True, lower=True)
+    upper_factor, inverse = factor_pallas(full_gram)
     basis_rows = jnp.dot(
         own_rows.reshape(-1, rank_width), inverse.T, precision=lax.Precision.HIGHEST
     )
-    return (basis_rows.reshape(own_count, 2 * rank_width), lower_factor.T)
+    return (basis_rows.reshape(own_count, 2 * rank_width), upper_factor)
 
 
 def solution(mesh):

time: 153 us -> 146 us (0.954)
  other arithmetic: 23.9 us -> 1.02 us
  Pallas kernels: 51.4 us -> 67.3 us
    another operation x4 -> x0, other arithmetic: 22.2 us -> none  [the longest x3 12.4 us: per_device(): lower_factor = jnp.linalg.cholesky(full_gram)]
    pallas_call x0 -> x1, Pallas kernels: none -> 16 us  [factor_pallas(): pl.pallas_call(factor_kernel, out_shape=(jax.ShapeDtypeStruct((size, size...]
where the time goes in v2:
time: 146 us
  Pallas kernels  67.3 us (46%)
  blocking collectives  35.1 us (24%)
  waiting for transfers between devices  18.2 us (12%)
  starting transfers between devices  15.6 us (11%)
  local copies, waits for them, and re-layouts  4.5 us (3%)
  matrix products  3.1 us (2%)
    pallas_call x1, Pallas kernels, sketch_pallas(): pl.pallas_call(sketch_kernel, grid=(sources // col_block,), in_specs=[pl....  51.4 us
    all_to_all x1, blocking collectives, from_everyone(): return lax.all_to_all(copies, axis, split_axis=0, concat_axis=0, tiled=True)  24.3 us
    pallas_call x1, Pallas kernels, factor_pallas(): pl.pallas_call(factor_kernel, out_shape=(jax.ShapeDtypeStruct((size, size...  16 us
    all_to_all x1, waiting for transfers between devices, sent_and_summed(): lax.all_to_all(tiles, axis, split_axis=0, concat_axis=0, tiled=True)  10.9 us
    all_to_all x1, blocking collectives, sent_and_summed(): lax.all_to_all(tiles, axis, split_axis=0, concat_axis=0, tiled=True)  10.8 us
    all_to_all x1, starting transfers between devices, sent_and_summed(): lax.all_to_all(tiles, axis, split_axis=0, concat_axis=0, tiled=True)  10.4 us
    all_to_all x1, waiting for transfers between devices, from_everyone(): return lax.all_to_all(copies, axis, split_axis=0, concat_axis=0, tiled=True)  7.3 us
    all_to_all x1, starting transfers between devices, from_everyone(): return lax.all_to_all(copies, axis, split_axis=0, concat_axis=0, tiled=True)  5.26 us
  transfers between devices with their start and end apart: 2, of which 2 were waited for; matrix products, arithmetic and copies ran while one was open for 1% of the time, Pallas kernels for 0%

profile of v2, /device:TPU:1, one launch (start us, length us, event | category | flops | bytes accessed | tf_op | source)
XLA Modules:
  0.0 145.6 jit_solution(7332247413258740495)
XLA Ops:
  0.6 0.0 copy-start.1
  0.6 0.8 bitcast_convert_fusion
  1.5 0.0 copy-done.1
  1.5 0.0 copy-start.2
  1.5 0.7 copy-done.2
  2.2 0.3 convolution_bitcast_fusion
  2.5 0.3 convolution_add_fusion.1
  2.8 0.0 copy-start.3
  2.8 1.1 convolution_add_fusion.coef_ref
  3.9 0.0 copy-done.3
  3.9 1.0 broadcast_in_dim.6.txy_ref
  4.9 51.4 %shard_map.77 = f32[512,256]{1,0:T(8,128)} custom-call(f32[2,512,128]{2,1,0:T(8,128)} %broadcast_in_dim.6.txy_ref, f32[2,2048]{1,0:T(2,128)} %sxy_ref.1, f32[64,2048]{1,0:T(8,128)} %convolution_add_fusion.coef_ref, bf16[2048,128]{1,0:T(8,128)(2,1)} %probe_ref.1), custom_call_target="tpu_custom_call" | custom-call | tf_op jit(solution)/shard_map/pallas_call | solution.py:93
  56.3 10.4 %all-to-all-start = ((f32[32,16,256]{2,1,0:T(8,128)}), f32[32,16,256]{2,1,0:T(8,128)S(1)}, u32[]{:S(2)}, u32[]{:S(2)}) async-start(f32[32,16,256]{2,1,0:T(8,128)} %bitcast.24), calls=%async_computation | async-start | bytes 1048576 | tf_op jit(solution)/shard_map/all_to_all | solution.py:155
  66.7 0.8 dynamic_slice.3
  67.4 10.9 %all-to-all-done = f32[32,16,256]{2,1,0:T(8,128)S(1)} async-done(((f32[32,16,256]{2,1,0:T(8,128)}), f32[32,16,256]{2,1,0:T(8,128)S(1)}, u32[]{:S(2)}, u32[]{:S(2)}) %all-to-all-start) | async-done | bytes 524320 | tf_op jit(solution)/shard_map/all_to_all | solution.py:155
  78.4 0.1 broadcast_multiply_fusion
  78.5 0.3 convolution_multiply_fusion
  78.8 10.8 %all_to_all.20 = f32[32,4,128]{2,1,0:T(4,128)S(1)} all-to-all(f32[32,4,128]{2,1,0:T(4,128)S(1)} %bitcast.26), channel_id=1, replica_groups=mesh['tgt'=16,'src'=32] {'src'}, dimensions={0} | all-to-all | bytes 131072 | tf_op jit(solution)/shard_map/all_to_all | solution.py:155
  89.6 24.3 %all_to_all.21 = f32[16,4,128]{2,1,0:T(4,128)S(1)} all-to-all(f32[16,4,128]{2,1,0:T(4,128)S(1)} %broadcast_in_dim.7), channel_id=1, replica_groups=mesh['tgt'=16,'src'=32] {'tgt'}, dimensions={0} | all-to-all | bytes 65536 | tf_op jit(solution)/shard_map/all_to_all | solution.py:161
  113.9 0.6 broadcast_in_dim.8
  114.6 5.3 %all-to-all-start.3 = ((f32[32,4,128]{2,1,0:T(4,128)}), f32[32,4,128]{2,1,0:T(4,128)S(1)}, u32[]{:S(2)}, u32[]{:S(2)}) async-start(f32[32,4,128]{2,1,0:T(4,128)} %broadcast_in_dim.8), calls=%async_computation.3 | async-start | bytes 131072 | tf_op jit(solution)/shard_map/all_to_all | solution.py:161
  119.8 0.1 mul.34
  119.9 0.1 mul.35
  120.0 7.3 %all-to-all-done.3 = f32[32,4,128]{2,1,0:T(4,128)S(1)} async-done(((f32[32,4,128]{2,1,0:T(4,128)}), f32[32,4,128]{2,1,0:T(4,128)S(1)}, u32[]{:S(2)}, u32[]{:S(2)}) %all-to-all-start.3) | async-done | bytes 65568 | tf_op jit(solution)/shard_map/all_to_all | solution.py:161
  127.3 0.0 copy-start
  127.3 0.6 copy-done
  127.9 16.0 %shard_map.78 = (f32[128,128]{1,0:T(8,128)}, f32[128,128]{1,0:T(8,128)}) custom-call(f32[128,128]{1,0:T(8,128)} %bitcast.25), custom_call_target="tpu_custom_call" | custom-call | tf_op jit(solution)/shard_map/pallas_call | solution.py:140
  143.9 1.1 fusion.4
  145.0 0.6 reshape.68
  (7 shorter events, 0.1 us)
Async XLA Ops:
  0.6 0.8 copy-start.1
  1.5 0.7 copy-start.2
  2.8 1.1 copy-start.3
  56.3 22.1 %all-to-all-start = ((f32[32,16,256]{2,1,0:T(8,128)}), f32[32,16,256]{2,1,0:T(8,128)S(1)}, u32[]{:S(2)}, u32[]{:S(2)}) async-start(f32[32,16,256]{2,1,0:T(8,128)} %bitcast.24), calls=%async_computation | async-start | bytes 1048576 | tf_op jit(solution)/shard_map/all_to_all | solution.py:155
  114.6 12.7 %all-to-all-start.3 = ((f32[32,4,128]{2,1,0:T(4,128)}), f32[32,4,128]{2,1,0:T(4,128)S(1)}, u32[]{:S(2)}, u32[]{:S(2)}) async-start(f32[32,4,128]{2,1,0:T(4,128)} %broadcast_in_dim.8), calls=%async_computation.3 | async-start | bytes 131072 | tf_op jit(solution)/shard_map/all_to_all | solution.py:161
  127.3 0.6 copy-start

commit v3 on v2

--- a/solution.py
+++ b/solution.py
@@ -34,7 +34,7 @@
     return cos_value, sin_value
 
 
-def sketch_kernel(txy_ref, sxy_ref, coef_ref, probe_ref, out_ref, re_scr, im_scr):
+def sketch_kernel(txy_ref, sxy_ref, table_ref, body_ref, probe_ref, out_ref, coef_ref, re_scr, im_scr):
     col_step = pl.program_id(0)
     rows = re_scr.shape[0]
     groups = re_scr.shape[1] // LANES
@@ -43,6 +43,19 @@
     @pl.when(col_step == 0)
     def _():
         out_ref[...] = jnp.zeros_like(out_ref)
+
+    table = table_ref[...]
+    bodies = table.shape[1]
+    one_hot = (
+        lax.broadcasted_iota(jnp.int32, (bodies, body_ref.shape[1]), 0) == body_ref[...]
+    ).astype(jnp.bfloat16)
+    high_part = table.astype(jnp.bfloat16)
+    rest_one = table - high_part.astype(jnp.float32)
+    middle_part = rest_one.astype(jnp.bfloat16)
+    low_part = (rest_one - middle_part.astype(jnp.float32)).astype(jnp.bfloat16)
+    picked = jnp.dot(high_part, one_hot, preferred_element_type=jnp.float32)
+    picked = picked + jnp.dot(middle_part, one_hot, preferred_element_type=jnp.float32)
+    coef_ref[...] = picked + jnp.dot(low_part, one_hot, preferred_element_type=jnp.float32)
 
     def one_sub(index, carry):
         row_at = pl.multiple_of((index // groups) * SUB_ROWS, SUB_ROWS)
@@ -84,29 +97,32 @@
     out_ref[:, rank:] += jnp.dot(im_scr[...], probe, preferred_element_type=jnp.float32)
 
 
-def sketch_pallas(target_xy, source_xy, picked, probe_matrix):
+def sketch_pallas(target_xy, source_xy, series_coef, body_of, probe_matrix):
     rows = target_xy.shape[1]
     sources = source_xy.shape[1]
     rank = probe_matrix.shape[1]
     col_block = min(COL_BLOCK, sources)
     txy = jnp.broadcast_to(target_xy[:, :, None], (2, rows, LANES))
+    table = series_coef.reshape(-1, series_coef.shape[2])
     return pl.pallas_call(
         sketch_kernel,
         grid=(sources // col_block,),
         in_specs=[
             pl.BlockSpec((2, rows, LANES), lambda j: (0, 0, 0)),
             pl.BlockSpec((2, col_block), lambda j: (0, j)),
-            pl.BlockSpec((picked.shape[0], col_block), lambda j: (0, j)),
+            pl.BlockSpec(table.shape, lambda j: (0, 0)),
+            pl.BlockSpec((1, col_block), lambda j: (0, j)),
             pl.BlockSpec((col_block, rank), lambda j: (j, 0)),
         ],
         out_specs=pl.BlockSpec((rows, 2 * rank), lambda j: (0, 0)),
         out_shape=jax.ShapeDtypeStruct((rows, 2 * rank), jnp.float32),
-        scratch_shapes=[pltpu.VMEM((rows, col_block), jnp.bfloat16),
+        scratch_shapes=[pltpu.VMEM((table.shape[0], col_block), jnp.float32),
+                        pltpu.VMEM((rows, col_block), jnp.bfloat16),
                         pltpu.VMEM((rows, col_block), jnp.bfloat16)],
-    )(txy, source_xy, picked, probe_matrix)
-
-
-def factor_kernel(gram_ref, upper_ref, inverse_ref):
+    )(txy, source_xy, table, body_of.reshape(1, sources), probe_matrix)
+
+
+def factor_kernel(gram_ref, rows_ref, upper_ref, basis_ref, inverse_ref):
     size = gram_ref.shape[0]
     upper_ref[...] = gram_ref[...]
     rows = lax.broadcasted_iota(jnp.int32, (size, size), 0)
@@ -133,15 +149,25 @@
 
     lax.fori_loop(0, size, step, 0)
     upper_ref[...] = jnp.where(rows <= cols, upper_ref[...], 0.0)
-
-
-def factor_pallas(gram):
+    inverse = inverse_ref[...]
+    for half in range(rows_ref.shape[1] // size):
+        basis_ref[:, half * size : (half + 1) * size] = lax.dot_general(
+            rows_ref[:, half * size : (half + 1) * size],
+            inverse,
+            (((1,), (1,)), ((), ())),
+            precision=lax.Precision.HIGHEST,
+            preferred_element_type=jnp.float32,
+        )
+
+
+def factor_pallas(gram, own_rows):
     size = gram.shape[0]
     return pl.pallas_call(
         factor_kernel,
         out_shape=(jax.ShapeDtypeStruct((size, size), jnp.float32),
-                   jax.ShapeDtypeStruct((size, size), jnp.float32)),
-    )(gram)
+                   jax.ShapeDtypeStruct(own_rows.shape, jnp.float32)),
+        scratch_shapes=[pltpu.VMEM((size, size), jnp.float32)],
+    )(gram, own_rows)
 
 
 def in_blocks(array, dim, count):
@@ -232,13 +258,12 @@
 
 def per_device(target_xy, source_xy, body_of, series_coef, probe_matrix, row_weight):
     rank_width = probe_matrix.shape[1]
-    picked = pick_coefficients(series_coef, body_of)
     rows_all = target_xy.shape[1]
     own_count = rows_all // lax.axis_size("src")
     scale_rows = float(2 * rows_all * lax.axis_size("tgt"))
     own_start = lax.axis_index("src") * own_count
     own_sum = sent_and_summed(
-        sketch_pallas(target_xy, source_xy, picked, probe_matrix),
+        sketch_pallas(target_xy, source_xy, series_coef, body_of, probe_matrix),
         "src",
         0,
     )
@@ -248,11 +273,8 @@
     gram_piece = sent_and_summed(local_gram, "src", 0)
     gram_piece = of_everyone(gram_piece, "tgt")
     full_gram = from_everyone(gram_piece, "src").reshape(rank_width, rank_width)
-    upper_factor, inverse = factor_pallas(full_gram)
-    basis_rows = jnp.dot(
-        own_rows.reshape(-1, rank_width), inverse.T, precision=lax.Precision.HIGHEST
-    )
-    return (basis_rows.reshape(own_count, 2 * rank_width), upper_factor)
+    upper_factor, basis_rows = factor_pallas(full_gram, own_rows)
+    return (basis_rows, upper_factor)
 
 
 def solution(mesh):

time: 146 us -> 141 us (0.966)
  blocking collectives: 35.1 us -> 47.6 us
  waiting for transfers between devices: 18.2 us -> 10.9 us
  starting transfers between devices: 15.6 us -> 10.4 us
  matrix products: 3.1 us -> 0.29 us
    all_to_all x1 -> x2, blocking collectives: 24.3 us -> 36.9 us  [from_everyone(): return lax.all_to_all(copies, axis, split_axis=0, concat_axis=0, tiled=True)]
    all_to_all x1 -> x0, waiting for transfers between devices: 7.3 us -> none  [from_everyone(): return lax.all_to_all(copies, axis, split_axis=0, concat_axis=0, tiled=True)]
    all_to_all x1 -> x0, starting transfers between devices: 5.26 us -> none  [from_everyone(): return lax.all_to_all(copies, axis, split_axis=0, concat_axis=0, tiled=True)]
    dot_general x4 -> x0, matrix products: 2.81 us -> none  [the longest x1 1.11 us: pick_coefficients(): jnp.dot(low_part, one_hot, preferred_element_type=jnp.float32)]
  transfers between devices with their start and end apart: 2 -> 1, of which waited for: 2 -> 1; matrix products, arithmetic and copies ran while one was open for 1% -> 1% of each run, Pallas kernels for 0% -> 0%
where the time goes in v3:
time: 141 us
  Pallas kernels  67.6 us (48%)
  blocking collectives  47.6 us (34%)
  waiting for transfers between devices  10.9 us (8%)
  starting transfers between devices  10.4 us (7%)
  local copies, waits for them, and re-layouts  3.06 us (2%)
    pallas_call x1, Pallas kernels, sketch_pallas(): pl.pallas_call(sketch_kernel, grid=(sources // col_block,), in_specs=[pl....  51.4 us
    all_to_all x2, blocking collectives, from_everyone(): return lax.all_to_all(copies, axis, split_axis=0, concat_axis=0, tiled=True)  36.9 us
    pallas_call x1, Pallas kernels, factor_pallas(): pl.pallas_call(factor_kernel, out_shape=(jax.ShapeDtypeStruct((size, size...  16.2 us
    all_to_all x1, waiting for transfers between devices, sent_and_summed(): lax.all_to_all(tiles, axis, split_axis=0, concat_axis=0, tiled=True)  10.9 us
    all_to_all x1, blocking collectives, sent_and_summed(): lax.all_to_all(tiles, axis, split_axis=0, concat_axis=0, tiled=True)  10.8 us
    all_to_all x1, starting transfers between devices, sent_and_summed(): lax.all_to_all(tiles, axis, split_axis=0, concat_axis=0, tiled=True)  10.4 us
  transfers between devices with their start and end apart: 1, of which 1 were waited for; matrix products, arithmetic and copies ran while one was open for 1% of the time, Pallas kernels for 0%

profile of v3, /device:TPU:1, one launch (start us, length us, event | category | flops | bytes accessed | tf_op | source)
XLA Modules:
  0.0 140.8 jit_solution(16118430664734584476)
XLA Ops:
  0.6 1.7 %broadcast_in_dim.6.txy_ref = f32[2,512,128]{2,1,0:T(8,128)} broadcast(f32[2,512]{1,0:T(2,128)} %param.6), dimensions={0,1} | broadcast | bytes 528384 | tf_op jit(solution)/shard_map/broadcast_in_dim | solution.py:105
  2.3 51.4 %shard_map.77 = f32[512,256]{1,0:T(8,128)} custom-call(f32[2,512,128]{2,1,0:T(8,128)} %broadcast_in_dim.6.txy_ref, f32[2,2048]{1,0:T(2,128)} %sxy_ref.1, f32[64,128]{1,0:T(8,128)} %bitcast.10, s32[1,2048]{1,0:T(1,128)} %bitcast.11, bf16[2048,128]{1,0:T(8,128)(2,1)} %probe_ref.1), custom_call_target="tpu_custom_call" | custom-call | tf_op jit(solution)/shard_map/pallas_call | solution.py:107
  53.7 10.4 %all-to-all-start = ((f32[32,16,256]{2,1,0:T(8,128)}), f32[32,16,256]{2,1,0:T(8,128)S(1)}, u32[]{:S(2)}, u32[]{:S(2)}) async-start(f32[32,16,256]{2,1,0:T(8,128)} %bitcast.7), calls=%async_computation | async-start | bytes 1048576 | tf_op jit(solution)/shard_map/all_to_all | solution.py:181
  64.1 0.8 dynamic_slice.3
  64.8 10.9 %all-to-all-done = f32[32,16,256]{2,1,0:T(8,128)S(1)} async-done(((f32[32,16,256]{2,1,0:T(8,128)}), f32[32,16,256]{2,1,0:T(8,128)S(1)}, u32[]{:S(2)}, u32[]{:S(2)}) %all-to-all-start) | async-done | bytes 524320 | tf_op jit(solution)/shard_map/all_to_all | solution.py:181
  75.8 0.1 broadcast_multiply_fusion.rows_ref
  75.9 0.0 copy-start
  75.9 0.6 copy-done
  76.5 0.3 convolution_multiply_fusion
  76.8 10.8 %all_to_all.20 = f32[32,4,128]{2,1,0:T(4,128)S(1)} all-to-all(f32[32,4,128]{2,1,0:T(4,128)S(1)} %bitcast.9), channel_id=1, replica_groups=mesh['tgt'=16,'src'=32] {'src'}, dimensions={0} | all-to-all | bytes 131072 | tf_op jit(solution)/shard_map/all_to_all | solution.py:181
  87.6 24.3 %all_to_all.21 = f32[16,4,128]{2,1,0:T(4,128)S(1)} all-to-all(f32[16,4,128]{2,1,0:T(4,128)S(1)} %broadcast_in_dim.14), channel_id=1, replica_groups=mesh['tgt'=16,'src'=32] {'tgt'}, dimensions={0} | all-to-all | bytes 65536 | tf_op jit(solution)/shard_map/all_to_all | solution.py:187
  112.0 12.6 %all_to_all.22 = f32[32,4,128]{2,1,0:T(4,128)} all-to-all(f32[32,4,128]{2,1,0:T(4,128)S(1)} %broadcast_in_dim.15), channel_id=1, replica_groups=mesh['tgt'=16,'src'=32] {'src'}, dimensions={0} | all-to-all | bytes 131072 | tf_op jit(solution)/shard_map/all_to_all | solution.py:187
  124.5 16.2 %shard_map.78 = (f32[128,128]{1,0:T(8,128)}, f32[16,256]{1,0:T(8,128)}) custom-call(f32[128,128]{1,0:T(8,128)} %bitcast.8, f32[16,256]{1,0:T(8,128)} %copy-done), custom_call_target="tpu_custom_call" | custom-call | tf_op jit(solution)/shard_map/pallas_call | solution.py:165
  (6 shorter events, 0.1 us)
Async XLA Ops:
  53.7 22.1 %all-to-all-start = ((f32[32,16,256]{2,1,0:T(8,128)}), f32[32,16,256]{2,1,0:T(8,128)S(1)}, u32[]{:S(2)}, u32[]{:S(2)}) async-start(f32[32,16,256]{2,1,0:T(8,128)} %bitcast.7), calls=%async_computation | async-start | bytes 1048576 | tf_op jit(solution)/shard_map/all_to_all | solution.py:181
  75.9 0.6 copy-start

commit v4 on v3

--- a/solution.py
+++ b/solution.py
@@ -34,7 +34,7 @@
     return cos_value, sin_value
 
 
-def sketch_kernel(txy_ref, sxy_ref, table_ref, body_ref, probe_ref, out_ref, coef_ref, re_scr, im_scr):
+def sketch_kernel(target_ref, sxy_ref, table_ref, body_ref, probe_ref, out_ref, txy_ref, coef_ref, re_scr, im_scr):
     col_step = pl.program_id(0)
     rows = re_scr.shape[0]
     groups = re_scr.shape[1] // LANES
@@ -43,6 +43,12 @@
     @pl.when(col_step == 0)
     def _():
         out_ref[...] = jnp.zeros_like(out_ref)
+        tile = jnp.zeros((8, rows), jnp.float32)
+        tile = jnp.where(lax.broadcasted_iota(jnp.int32, (8, rows), 0) == 0, target_ref[0:1, :], tile)
+        tile = jnp.where(lax.broadcasted_iota(jnp.int32, (8, rows), 0) == 1, target_ref[1:2, :], tile)
+        columns = jnp.transpose(tile)
+        txy_ref[0] = jnp.broadcast_to(columns[:, 0:1], (rows, LANES))
+        txy_ref[1] = jnp.broadcast_to(columns[:, 1:2], (rows, LANES))
 
     table = table_ref[...]
     bodies = table.shape[1]
@@ -102,13 +108,12 @@
     sources = source_xy.shape[1]
     rank = probe_matrix.shape[1]
     col_block = min(COL_BLOCK, sources)
-    txy = jnp.broadcast_to(target_xy[:, :, None], (2, rows, LANES))
     table = series_coef.reshape(-1, series_coef.shape[2])
     return pl.pallas_call(
         sketch_kernel,
         grid=(sources // col_block,),
         in_specs=[
-            pl.BlockSpec((2, rows, LANES), lambda j: (0, 0, 0)),
+            pl.BlockSpec((2, rows), lambda j: (0, 0)),
             pl.BlockSpec((2, col_block), lambda j: (0, j)),
             pl.BlockSpec(table.shape, lambda j: (0, 0)),
             pl.BlockSpec((1, col_block), lambda j: (0, j)),
@@ -116,10 +121,11 @@
         ],
         out_specs=pl.BlockSpec((rows, 2 * rank), lambda j: (0, 0)),
         out_shape=jax.ShapeDtypeStruct((rows, 2 * rank), jnp.float32),
-        scratch_shapes=[pltpu.VMEM((table.shape[0], col_block), jnp.float32),
+        scratch_shapes=[pltpu.VMEM((2, rows, LANES), jnp.float32),
+                        pltpu.VMEM((table.shape[0], col_block), jnp.float32),
                         pltpu.VMEM((rows, col_block), jnp.bfloat16),
                         pltpu.VMEM((rows, col_block), jnp.bfloat16)],
-    )(txy, source_xy, table, body_of.reshape(1, sources), probe_matrix)
+    )(target_xy, source_xy, table, body_of.reshape(1, sources), probe_matrix)
 
 
 def factor_kernel(gram_ref, rows_ref, upper_ref, basis_ref, inverse_ref):

time: 141 us -> 140 us (level)
  local copies, waits for them, and re-layouts: 3.06 us -> 1.38 us
    broadcast_in_dim x1 -> x0, local copies, waits for them, and re-layouts: 1.68 us -> none  [sketch_pallas(): txy = jnp.broadcast_to(target_xy[:, :, None], (2, rows, LANES))]
where the time goes in v4:
time: 140 us; the launch traced here: 139 us
  Pallas kernels  67.7 us (48%)
  blocking collectives  47.6 us (34%)
  waiting for transfers between devices  10.9 us (8%)
  starting transfers between devices  10.4 us (7%)
    pallas_call x1, Pallas kernels, sketch_pallas(): pl.pallas_call(sketch_kernel, grid=(sources // col_block,), in_specs=[pl....  51.5 us
    all_to_all x2, blocking collectives, from_everyone(): return lax.all_to_all(copies, axis, split_axis=0, concat_axis=0, tiled=True)  36.9 us
    pallas_call x1, Pallas kernels, factor_pallas(): pl.pallas_call(factor_kernel, out_shape=(jax.ShapeDtypeStruct((size, size...  16.2 us
    all_to_all x1, waiting for transfers between devices, sent_and_summed(): lax.all_to_all(tiles, axis, split_axis=0, concat_axis=0, tiled=True)  10.9 us
    all_to_all x1, blocking collectives, sent_and_summed(): lax.all_to_all(tiles, axis, split_axis=0, concat_axis=0, tiled=True)  10.8 us
    all_to_all x1, starting transfers between devices, sent_and_summed(): lax.all_to_all(tiles, axis, split_axis=0, concat_axis=0, tiled=True)  10.4 us
  transfers between devices with their start and end apart: 1, of which 1 were waited for; matrix products, arithmetic and copies ran while one was open for 1% of the time, Pallas kernels for 0%

profile of v4, /device:TPU:1, one launch (start us, length us, event | category | flops | bytes accessed | tf_op | source)
XLA Modules:
  0.0 139.2 jit_solution(5591211600295054494)
XLA Ops:
  0.6 51.5 %shard_map.77 = f32[512,256]{1,0:T(8,128)} custom-call(f32[2,512]{1,0:T(2,128)} %target_ref.1, f32[2,2048]{1,0:T(2,128)} %sxy_ref.1, f32[64,128]{1,0:T(8,128)} %bitcast.10, s32[1,2048]{1,0:T(1,128)} %bitcast.11, bf16[2048,128]{1,0:T(8,128)(2,1)} %probe_ref.1), custom_call_target="tpu_custom_call" | custom-call | tf_op jit(solution)/shard_map/pallas_call | solution.py:112
  52.1 10.4 %all-to-all-start = ((f32[32,16,256]{2,1,0:T(8,128)}), f32[32,16,256]{2,1,0:T(8,128)S(1)}, u32[]{:S(2)}, u32[]{:S(2)}) async-start(f32[32,16,256]{2,1,0:T(8,128)} %bitcast.7), calls=%async_computation | async-start | bytes 1048576 | tf_op jit(solution)/shard_map/all_to_all | solution.py:187
  62.5 0.8 dynamic_slice.3
  63.3 10.9 %all-to-all-done = f32[32,16,256]{2,1,0:T(8,128)S(1)} async-done(((f32[32,16,256]{2,1,0:T(8,128)}), f32[32,16,256]{2,1,0:T(8,128)S(1)}, u32[]{:S(2)}, u32[]{:S(2)}) %all-to-all-start) | async-done | bytes 524320 | tf_op jit(solution)/shard_map/all_to_all | solution.py:187
  74.3 0.1 broadcast_multiply_fusion.rows_ref
  74.3 0.0 copy-start
  74.3 0.6 copy-done
  74.9 0.3 convolution_multiply_fusion
  75.2 10.8 %all_to_all.20 = f32[32,4,128]{2,1,0:T(4,128)S(1)} all-to-all(f32[32,4,128]{2,1,0:T(4,128)S(1)} %bitcast.9), channel_id=1, replica_groups=mesh['tgt'=16,'src'=32] {'src'}, dimensions={0} | all-to-all | bytes 131072 | tf_op jit(solution)/shard_map/all_to_all | solution.py:187
  86.0 24.3 %all_to_all.21 = f32[16,4,128]{2,1,0:T(4,128)S(1)} all-to-all(f32[16,4,128]{2,1,0:T(4,128)S(1)} %broadcast_in_dim.7), channel_id=1, replica_groups=mesh['tgt'=16,'src'=32] {'tgt'}, dimensions={0} | all-to-all | bytes 65536 | tf_op jit(solution)/shard_map/all_to_all | solution.py:193
  110.4 12.6 %all_to_all.22 = f32[32,4,128]{2,1,0:T(4,128)} all-to-all(f32[32,4,128]{2,1,0:T(4,128)S(1)} %broadcast_in_dim.8), channel_id=1, replica_groups=mesh['tgt'=16,'src'=32] {'src'}, dimensions={0} | all-to-all | bytes 131072 | tf_op jit(solution)/shard_map/all_to_all | solution.py:193
  122.9 16.2 %shard_map.78 = (f32[128,128]{1,0:T(8,128)}, f32[16,256]{1,0:T(8,128)}) custom-call(f32[128,128]{1,0:T(8,128)} %bitcast.8, f32[16,256]{1,0:T(8,128)} %copy-done), custom_call_target="tpu_custom_call" | custom-call | tf_op jit(solution)/shard_map/pallas_call | solution.py:171
  (6 shorter events, 0.1 us)
Async XLA Ops:
  52.1 22.1 %all-to-all-start = ((f32[32,16,256]{2,1,0:T(8,128)}), f32[32,16,256]{2,1,0:T(8,128)S(1)}, u32[]{:S(2)}, u32[]{:S(2)}) async-start(f32[32,16,256]{2,1,0:T(8,128)} %bitcast.7), calls=%async_computation | async-start | bytes 1048576 | tf_op jit(solution)/shard_map/all_to_all | solution.py:187
  74.3 0.6 copy-start

commit v5 on v4

--- a/solution.py
+++ b/solution.py
@@ -1,3 +1,4 @@
+import functools
 import math
 
 import jax
@@ -34,7 +35,7 @@
     return cos_value, sin_value
 
 
-def sketch_kernel(target_ref, sxy_ref, table_ref, body_ref, probe_ref, out_ref, txy_ref, coef_ref, re_scr, im_scr):
+def sketch_kernel(target_ref, sxy_ref, table_ref, body_ref, probe_ref, out_ref, txy_ref, coef_ref, re_scr, im_scr, *, part, parts, owners):
     col_step = pl.program_id(0)
     rows = re_scr.shape[0]
     groups = re_scr.shape[1] // LANES
@@ -43,12 +44,17 @@
     @pl.when(col_step == 0)
     def _():
         out_ref[...] = jnp.zeros_like(out_ref)
-        tile = jnp.zeros((8, rows), jnp.float32)
-        tile = jnp.where(lax.broadcasted_iota(jnp.int32, (8, rows), 0) == 0, target_ref[0:1, :], tile)
-        tile = jnp.where(lax.broadcasted_iota(jnp.int32, (8, rows), 0) == 1, target_ref[1:2, :], tile)
+        all_rows = target_ref.shape[1]
+        tile = jnp.zeros((8, all_rows), jnp.float32)
+        tile = jnp.where(lax.broadcasted_iota(jnp.int32, (8, all_rows), 0) == 0, target_ref[0:1, :], tile)
+        tile = jnp.where(lax.broadcasted_iota(jnp.int32, (8, all_rows), 0) == 1, target_ref[1:2, :], tile)
         columns = jnp.transpose(tile)
-        txy_ref[0] = jnp.broadcast_to(columns[:, 0:1], (rows, LANES))
-        txy_ref[1] = jnp.broadcast_to(columns[:, 1:2], (rows, LANES))
+        piece = all_rows // (owners * parts)
+        for block in range(owners):
+            start = block * piece * parts + part * piece
+            picked_rows = columns[start : start + piece, :]
+            txy_ref[0, block * piece : (block + 1) * piece, :] = jnp.broadcast_to(picked_rows[:, 0:1], (piece, LANES))
+            txy_ref[1, block * piece : (block + 1) * piece, :] = jnp.broadcast_to(picked_rows[:, 1:2], (piece, LANES))
 
     table = table_ref[...]
     bodies = table.shape[1]
@@ -103,17 +109,17 @@
     out_ref[:, rank:] += jnp.dot(im_scr[...], probe, preferred_element_type=jnp.float32)
 
 
-def sketch_pallas(target_xy, source_xy, series_coef, body_of, probe_matrix):
-    rows = target_xy.shape[1]
+def sketch_pallas(target_xy, source_xy, series_coef, body_of, probe_matrix, part, parts, owners):
+    rows = target_xy.shape[1] // parts
     sources = source_xy.shape[1]
     rank = probe_matrix.shape[1]
     col_block = min(COL_BLOCK, sources)
     table = series_coef.reshape(-1, series_coef.shape[2])
     return pl.pallas_call(
-        sketch_kernel,
+        functools.partial(sketch_kernel, part=part, parts=parts, owners=owners),
         grid=(sources // col_block,),
         in_specs=[
-            pl.BlockSpec((2, rows), lambda j: (0, 0)),
+            pl.BlockSpec((2, target_xy.shape[1]), lambda j: (0, 0)),
             pl.BlockSpec((2, col_block), lambda j: (0, j)),
             pl.BlockSpec(table.shape, lambda j: (0, 0)),
             pl.BlockSpec((1, col_block), lambda j: (0, j)),
@@ -268,10 +274,17 @@
     own_count = rows_all // lax.axis_size("src")
     scale_rows = float(2 * rows_all * lax.axis_size("tgt"))
     own_start = lax.axis_index("src") * own_count
-    own_sum = sent_and_summed(
-        sketch_pallas(target_xy, source_xy, series_coef, body_of, probe_matrix),
-        "src",
-        0,
+    parts = 2
+    own_sum = jnp.concatenate(
+        [
+            sent_and_summed(
+                sketch_pallas(target_xy, source_xy, series_coef, body_of, probe_matrix, part, parts, lax.axis_size("src")),
+                "src",
+                0,
+            )
+            for part in range(parts)
+        ],
+        axis=0,
     )
     own_weight = lax.dynamic_slice_in_dim(row_weight, own_start, own_count, 0)
     own_rows = own_sum * own_weight[:, None]

time: 140 us -> 148 us (1.057)
  starting transfers between devices: 10.4 us -> 17.9 us
  Pallas kernels: 67.7 us -> 70.9 us
  waiting for transfers between devices: 10.9 us -> 8.16 us
    all_to_all x1 -> x2, starting transfers between devices: 10.4 us -> 17.9 us  [sent_and_summed(): lax.all_to_all(tiles, axis, split_axis=0, concat_axis=0, tiled=True)]
    pallas_call x1 -> x2, Pallas kernels: 51.5 us -> 54.7 us  [sketch_pallas(): pl.pallas_call(functools.partial(sketch_kernel, part=part, parts=parts, o...]
    all_to_all x1 -> x2, waiting for transfers between devices: 10.9 us -> 8.16 us  [sent_and_summed(): lax.all_to_all(tiles, axis, split_axis=0, concat_axis=0, tiled=True)]
  transfers between devices with their start and end apart: 1 -> 2, of which waited for: 1 -> 1; matrix products, arithmetic and copies ran while one was open for 1% -> 1% of each run, Pallas kernels for 0% -> 19%
where the time goes in v5:
time: 148 us; the launch traced here: 147 us
  Pallas kernels  70.9 us (48%)
  blocking collectives  47.7 us (32%)
  starting transfers between devices  17.9 us (12%)
  waiting for transfers between devices  8.16 us (6%)
    pallas_call x2, Pallas kernels, sketch_pallas(): pl.pallas_call(functools.partial(sketch_kernel, part=part, parts=parts, o...  54.7 us
    all_to_all x2, blocking collectives, from_everyone(): return lax.all_to_all(copies, axis, split_axis=0, concat_axis=0, tiled=True)  36.8 us
    all_to_all x2, starting transfers between devices, sent_and_summed(): lax.all_to_all(tiles, axis, split_axis=0, concat_axis=0, tiled=True)  17.9 us
    pallas_call x1, Pallas kernels, factor_pallas(): pl.pallas_call(factor_kernel, out_shape=(jax.ShapeDtypeStruct((size, size...  16.2 us
    all_to_all x1, blocking collectives, sent_and_summed(): lax.all_to_all(tiles, axis, split_axis=0, concat_axis=0, tiled=True)  10.8 us
    all_to_all x2, waiting for transfers between devices, sent_and_summed(): lax.all_to_all(tiles, axis, split_axis=0, concat_axis=0, tiled=True)  8.16 us
  transfers between devices with their start and end apart: 2, of which 1 were waited for; matrix products, arithmetic and copies ran while one was open for 1% of the time, Pallas kernels for 19%

profile of v5, /device:TPU:1, one launch (start us, length us, event | category | flops | bytes accessed | tf_op | source)
XLA Modules:
  0.0 147.2 jit_solution(9648462785762238913)
XLA Ops:
  0.6 27.3 %shard_map.78 = f32[256,256]{1,0:T(8,128)} custom-call(f32[2,512]{1,0:T(2,128)} %target_ref.3, f32[2,2048]{1,0:T(2,128)} %sxy_ref.3, f32[64,128]{1,0:T(8,128)} %bitcast.12, s32[1,2048]{1,0:T(1,128)} %bitcast.14, bf16[2048,128]{1,0:T(8,128)(2,1)} %probe_ref.3), custom_call_target="tpu_custom_call" | custom-call | tf_op jit(solution)/shard_map/pallas_call | solution.py:118
  28.0 10.4 %all-to-all-start.1 = ((f32[32,8,256]{2,1,0:T(8,128)}), f32[32,8,256]{2,1,0:T(8,128)S(1)}, u32[]{:S(2)}, u32[]{:S(2)}) async-start(f32[32,8,256]{2,1,0:T(8,128)} %bitcast.9), calls=%async_computation.1 | async-start | bytes 524288 | tf_op jit(solution)/shard_map/all_to_all | solution.py:193
  38.3 27.3 %shard_map.77 = f32[256,256]{1,0:T(8,128)} custom-call(f32[2,512]{1,0:T(2,128)} %target_ref.3, f32[2,2048]{1,0:T(2,128)} %sxy_ref.3, f32[64,128]{1,0:T(8,128)} %bitcast.13, s32[1,2048]{1,0:T(1,128)} %bitcast.15, bf16[2048,128]{1,0:T(8,128)(2,1)} %probe_ref.3), custom_call_target="tpu_custom_call" | custom-call | tf_op jit(solution)/shard_map/pallas_call | solution.py:118
  65.7 0.0 all-to-all-done.1
  65.7 7.5 %all-to-all-start = ((f32[32,8,256]{2,1,0:T(8,128)}), f32[32,8,256]{2,1,0:T(8,128)S(1)}, u32[]{:S(2)}, u32[]{:S(2)}) async-start(f32[32,8,256]{2,1,0:T(8,128)} %bitcast.8), calls=%async_computation | async-start | bytes 524288 | tf_op jit(solution)/shard_map/all_to_all | solution.py:193
  73.2 0.8 dynamic_slice.3
  74.0 8.2 %all-to-all-done = f32[32,8,256]{2,1,0:T(8,128)S(1)} async-done(((f32[32,8,256]{2,1,0:T(8,128)}), f32[32,8,256]{2,1,0:T(8,128)S(1)}, u32[]{:S(2)}, u32[]{:S(2)}) %all-to-all-start) | async-done | bytes 262176 | tf_op jit(solution)/shard_map/all_to_all | solution.py:193
  82.2 0.1 maximum_multiply_fusion.rows_ref
  82.2 0.0 copy-start
  82.2 0.6 copy-done
  82.8 0.3 convolution_multiply_fusion
  83.1 10.8 %all_to_all.25 = f32[32,4,128]{2,1,0:T(4,128)S(1)} all-to-all(f32[32,4,128]{2,1,0:T(4,128)S(1)} %bitcast.11), channel_id=1, replica_groups=mesh['tgt'=16,'src'=32] {'src'}, dimensions={0} | all-to-all | bytes 131072 | tf_op jit(solution)/shard_map/all_to_all | solution.py:193
  94.0 24.3 %all_to_all.26 = f32[16,4,128]{2,1,0:T(4,128)S(1)} all-to-all(f32[16,4,128]{2,1,0:T(4,128)S(1)} %broadcast_in_dim.7), channel_id=1, replica_groups=mesh['tgt'=16,'src'=32] {'tgt'}, dimensions={0} | all-to-all | bytes 65536 | tf_op jit(solution)/shard_map/all_to_all | solution.py:199
  118.4 12.6 %all_to_all.27 = f32[32,4,128]{2,1,0:T(4,128)} all-to-all(f32[32,4,128]{2,1,0:T(4,128)S(1)} %broadcast_in_dim.8), channel_id=1, replica_groups=mesh['tgt'=16,'src'=32] {'src'}, dimensions={0} | all-to-all | bytes 131072 | tf_op jit(solution)/shard_map/all_to_all | solution.py:199
  130.9 16.2 %shard_map.79 = (f32[128,128]{1,0:T(8,128)}, f32[16,256]{1,0:T(8,128)}) custom-call(f32[128,128]{1,0:T(8,128)} %bitcast.10, f32[16,256]{1,0:T(8,128)} %copy-done), custom_call_target="tpu_custom_call" | custom-call | tf_op jit(solution)/shard_map/pallas_call | solution.py:177
  (7 shorter events, 0.2 us)
Async XLA Ops:
  28.0 37.7 %all-to-all-start.1 = ((f32[32,8,256]{2,1,0:T(8,128)}), f32[32,8,256]{2,1,0:T(8,128)S(1)}, u32[]{:S(2)}, u32[]{:S(2)}) async-start(f32[32,8,256]{2,1,0:T(8,128)} %bitcast.9), calls=%async_computation.1 | async-start | bytes 524288 | tf_op jit(solution)/shard_map/all_to_all | solution.py:193
  65.7 16.5 %all-to-all-start = ((f32[32,8,256]{2,1,0:T(8,128)}), f32[32,8,256]{2,1,0:T(8,128)S(1)}, u32[]{:S(2)}, u32[]{:S(2)}) async-start(f32[32,8,256]{2,1,0:T(8,128)} %bitcast.8), calls=%async_computation | async-start | bytes 524288 | tf_op jit(solution)/shard_map/all_to_all | solution.py:193
  82.2 0.6 copy-start

commit v6 on v4

--- a/solution.py
+++ b/solution.py
@@ -34,7 +34,7 @@
     return cos_value, sin_value
 
 
-def sketch_kernel(target_ref, sxy_ref, table_ref, body_ref, probe_ref, out_ref, txy_ref, coef_ref, re_scr, im_scr):
+def sketch_kernel(target_ref, weight_ref, sxy_ref, table_ref, body_ref, probe_ref, out_ref, txy_ref, weight_scr, coef_ref, re_scr, im_scr):
     col_step = pl.program_id(0)
     rows = re_scr.shape[0]
     groups = re_scr.shape[1] // LANES
@@ -46,9 +46,11 @@
         tile = jnp.zeros((8, rows), jnp.float32)
         tile = jnp.where(lax.broadcasted_iota(jnp.int32, (8, rows), 0) == 0, target_ref[0:1, :], tile)
         tile = jnp.where(lax.broadcasted_iota(jnp.int32, (8, rows), 0) == 1, target_ref[1:2, :], tile)
+        tile = jnp.where(lax.broadcasted_iota(jnp.int32, (8, rows), 0) == 2, weight_ref[...], tile)
         columns = jnp.transpose(tile)
         txy_ref[0] = jnp.broadcast_to(columns[:, 0:1], (rows, LANES))
         txy_ref[1] = jnp.broadcast_to(columns[:, 1:2], (rows, LANES))
+        weight_scr[...] = jnp.broadcast_to(columns[:, 2:3], (rows, LANES))
 
     table = table_ref[...]
     bodies = table.shape[1]
@@ -102,8 +104,14 @@
     out_ref[:, :rank] += jnp.dot(re_scr[...], probe, preferred_element_type=jnp.float32)
     out_ref[:, rank:] += jnp.dot(im_scr[...], probe, preferred_element_type=jnp.float32)
 
-
-def sketch_pallas(target_xy, source_xy, series_coef, body_of, probe_matrix):
+    @pl.when(col_step == pl.num_programs(0) - 1)
+    def _():
+        weight = weight_scr[...]
+        out_ref[:, :rank] = out_ref[:, :rank] * weight
+        out_ref[:, rank:] = out_ref[:, rank:] * weight
+
+
+def sketch_pallas(target_xy, row_weight, source_xy, series_coef, body_of, probe_matrix):
     rows = target_xy.shape[1]
     sources = source_xy.shape[1]
     rank = probe_matrix.shape[1]
@@ -114,6 +122,7 @@
         grid=(sources // col_block,),
         in_specs=[
             pl.BlockSpec((2, rows), lambda j: (0, 0)),
+            pl.BlockSpec((1, rows), lambda j: (0, 0)),
             pl.BlockSpec((2, col_block), lambda j: (0, j)),
             pl.BlockSpec(table.shape, lambda j: (0, 0)),
             pl.BlockSpec((1, col_block), lambda j: (0, j)),
@@ -122,10 +131,11 @@
         out_specs=pl.BlockSpec((rows, 2 * rank), lambda j: (0, 0)),
         out_shape=jax.ShapeDtypeStruct((rows, 2 * rank), jnp.float32),
         scratch_shapes=[pltpu.VMEM((2, rows, LANES), jnp.float32),
+                        pltpu.VMEM((rows, LANES), jnp.float32),
                         pltpu.VMEM((table.shape[0], col_block), jnp.float32),
                         pltpu.VMEM((rows, col_block), jnp.bfloat16),
                         pltpu.VMEM((rows, col_block), jnp.bfloat16)],
-    )(target_xy, source_xy, table, body_of.reshape(1, sources), probe_matrix)
+    )(target_xy, row_weight.reshape(1, rows), source_xy, table, body_of.reshape(1, sources), probe_matrix)
 
 
 def factor_kernel(gram_ref, rows_ref, upper_ref, basis_ref, inverse_ref):
@@ -153,7 +163,7 @@
         inverse_ref[pl.ds(j, 1), :] = pivot_right
         return carry
 
-    lax.fori_loop(0, size, step, 0)
+    lax.fori_loop(0, size, step, 0, unroll=2)
     upper_ref[...] = jnp.where(rows <= cols, upper_ref[...], 0.0)
     inverse = inverse_ref[...]
     for half in range(rows_ref.shape[1] // size):
@@ -267,14 +277,12 @@
     rows_all = target_xy.shape[1]
     own_count = rows_all // lax.axis_size("src")
     scale_rows = float(2 * rows_all * lax.axis_size("tgt"))
-    own_start = lax.axis_index("src") * own_count
     own_sum = sent_and_summed(
-        sketch_pallas(target_xy, source_xy, series_coef, body_of, probe_matrix),
+        sketch_pallas(target_xy, row_weight, source_xy, series_coef, body_of, probe_matrix),
         "src",
         0,
     )
-    own_weight = lax.dynamic_slice_in_dim(row_weight, own_start, own_count, 0)
-    own_rows = own_sum * own_weight[:, None]
+    own_rows = own_sum
     local_gram = gram_of(own_rows, scale_rows)
     gram_piece = sent_and_summed(local_gram, "src", 0)
     gram_piece = of_everyone(gram_piece, "tgt")

time: 140 us -> 140 us (level)
  blocking collectives: 47.6 us -> 69.7 us
  waiting for transfers between devices: 10.9 us -> 0 us
  starting transfers between devices: 10.4 us -> 0 us
    all_to_all x1 -> x2, blocking collectives: 10.8 us -> 32.8 us  [sent_and_summed(): lax.all_to_all(tiles, axis, split_axis=0, concat_axis=0, tiled=True)]
    all_to_all x1 -> x0, waiting for transfers between devices: 10.9 us -> none  [sent_and_summed(): lax.all_to_all(tiles, axis, split_axis=0, concat_axis=0, tiled=True)]
    all_to_all x1 -> x0, starting transfers between devices: 10.4 us -> none  [sent_and_summed(): lax.all_to_all(tiles, axis, split_axis=0, concat_axis=0, tiled=True)]
  transfers between devices with their start and end apart: 1 -> 0, of which waited for: 1 -> 0; matrix products, arithmetic and copies ran while one was open for 1% -> 0% of each run, Pallas kernels for 0% -> 0%
where the time goes in v6:
time: 140 us; the launch traced here: 139 us
  blocking collectives  69.7 us (50%)
  Pallas kernels  67.8 us (48%)
    pallas_call x1, Pallas kernels, sketch_pallas(): pl.pallas_call(sketch_kernel, grid=(sources // col_block,), in_specs=[pl....  51.7 us
    all_to_all x2, blocking collectives, from_everyone(): return lax.all_to_all(copies, axis, split_axis=0, concat_axis=0, tiled=True)  36.9 us
    all_to_all x2, blocking collectives, sent_and_summed(): lax.all_to_all(tiles, axis, split_axis=0, concat_axis=0, tiled=True)  32.8 us
    pallas_call x1, Pallas kernels, factor_pallas(): pl.pallas_call(factor_kernel, out_shape=(jax.ShapeDtypeStruct((size, size...  16.1 us

profile of v6, /device:TPU:1, one launch (start us, length us, event | category | flops | bytes accessed | tf_op | source)
XLA Modules:
  0.0 139.2 jit_solution(8811035532984637893)
XLA Ops:
  0.6 51.7 %shard_map.77 = f32[512,256]{1,0:T(8,128)} custom-call(f32[2,512]{1,0:T(2,128)} %target_ref.1, f32[1,512]{1,0:T(1,128)} %bitcast.13, f32[2,2048]{1,0:T(2,128)} %sxy_ref.1, f32[64,128]{1,0:T(8,128)} %bitcast.11, s32[1,2048]{1,0:T(1,128)} %bitcast.12, bf16[2048,128]{1,0:T(8,128)(2,1)} %probe_ref.1), custom_call_target="tpu_custom_call" | custom-call | tf_op jit(solution)/shard_map/pallas_call | solution.py:120
  52.3 22.1 %all_to_all.20 = f32[32,16,256]{2,1,0:T(8,128)S(1)} all-to-all(f32[32,16,256]{2,1,0:T(8,128)} %bitcast.8), channel_id=1, replica_groups=mesh['tgt'=16,'src'=32] {'src'}, dimensions={0} | all-to-all | bytes 1048576 | tf_op jit(solution)/shard_map/all_to_all | solution.py:197
  74.4 0.0 copy-start
  74.4 0.6 copy-done
  75.0 0.3 convolution_multiply_fusion
  75.3 10.8 %all_to_all.21 = f32[32,4,128]{2,1,0:T(4,128)S(1)} all-to-all(f32[32,4,128]{2,1,0:T(4,128)S(1)} %bitcast.10), channel_id=1, replica_groups=mesh['tgt'=16,'src'=32] {'src'}, dimensions={0} | all-to-all | bytes 131072 | tf_op jit(solution)/shard_map/all_to_all | solution.py:197
  86.1 24.3 %all_to_all.22 = f32[16,4,128]{2,1,0:T(4,128)S(1)} all-to-all(f32[16,4,128]{2,1,0:T(4,128)S(1)} %broadcast_in_dim.6), channel_id=1, replica_groups=mesh['tgt'=16,'src'=32] {'tgt'}, dimensions={0} | all-to-all | bytes 65536 | tf_op jit(solution)/shard_map/all_to_all | solution.py:203
  110.5 12.6 %all_to_all.23 = f32[32,4,128]{2,1,0:T(4,128)} all-to-all(f32[32,4,128]{2,1,0:T(4,128)S(1)} %broadcast_in_dim.7), channel_id=1, replica_groups=mesh['tgt'=16,'src'=32] {'src'}, dimensions={0} | all-to-all | bytes 131072 | tf_op jit(solution)/shard_map/all_to_all | solution.py:203
  123.0 16.1 %shard_map.78 = (f32[128,128]{1,0:T(8,128)}, f32[16,256]{1,0:T(8,128)}) custom-call(f32[128,128]{1,0:T(8,128)} %bitcast.9, f32[16,256]{1,0:T(8,128)} %copy-done), custom_call_target="tpu_custom_call" | custom-call | tf_op jit(solution)/shard_map/pallas_call | solution.py:181
  (6 shorter events, 0.1 us)
Async XLA Ops:
  74.4 0.6 copy-start

commit v7 on v4

--- a/solution.py
+++ b/solution.py
@@ -10,7 +10,7 @@
 NTERMS = 32
 SUB_ROWS = 64
 LANES = 128
-COL_BLOCK = 512
+COL_BLOCK = 1024
 
 
 def cos_and_sin(angle):

time: 140 us -> 139 us (level)
  no operation moved by 1% of the time
where the time goes in v7:
time: 139 us
  Pallas kernels  67.1 us (48%)
  blocking collectives  47.6 us (34%)
  waiting for transfers between devices  10.9 us (8%)
  starting transfers between devices  10.4 us (7%)
    pallas_call x1, Pallas kernels, sketch_pallas(): pl.pallas_call(sketch_kernel, grid=(sources // col_block,), in_specs=[pl....  50.9 us
    all_to_all x2, blocking collectives, from_everyone(): return lax.all_to_all(copies, axis, split_axis=0, concat_axis=0, tiled=True)  36.8 us
    pallas_call x1, Pallas kernels, factor_pallas(): pl.pallas_call(factor_kernel, out_shape=(jax.ShapeDtypeStruct((size, size...  16.2 us
    all_to_all x1, waiting for transfers between devices, sent_and_summed(): lax.all_to_all(tiles, axis, split_axis=0, concat_axis=0, tiled=True)  10.9 us
    all_to_all x1, blocking collectives, sent_and_summed(): lax.all_to_all(tiles, axis, split_axis=0, concat_axis=0, tiled=True)  10.8 us
    all_to_all x1, starting transfers between devices, sent_and_summed(): lax.all_to_all(tiles, axis, split_axis=0, concat_axis=0, tiled=True)  10.4 us
  transfers between devices with their start and end apart: 1, of which 1 were waited for; matrix products, arithmetic and copies ran while one was open for 1% of the time, Pallas kernels for 0%

profile of v7, /device:TPU:1, one launch (start us, length us, event | category | flops | bytes accessed | tf_op | source)
XLA Modules:
  0.0 138.6 jit_solution(7349480579287569623)
XLA Ops:
  0.6 50.9 %shard_map.77 = f32[512,256]{1,0:T(8,128)} custom-call(f32[2,512]{1,0:T(2,128)} %target_ref.1, f32[2,2048]{1,0:T(2,128)} %sxy_ref.1, f32[64,128]{1,0:T(8,128)} %bitcast.10, s32[1,2048]{1,0:T(1,128)} %bitcast.11, bf16[2048,128]{1,0:T(8,128)(2,1)} %probe_ref.1), custom_call_target="tpu_custom_call" | custom-call | tf_op jit(solution)/shard_map/pallas_call | solution.py:112
  51.5 10.4 %all-to-all-start = ((f32[32,16,256]{2,1,0:T(8,128)}), f32[32,16,256]{2,1,0:T(8,128)S(1)}, u32[]{:S(2)}, u32[]{:S(2)}) async-start(f32[32,16,256]{2,1,0:T(8,128)} %bitcast.7), calls=%async_computation | async-start | bytes 1048576 | tf_op jit(solution)/shard_map/all_to_all | solution.py:187
  61.9 0.8 dynamic_slice.3
  62.7 10.9 %all-to-all-done = f32[32,16,256]{2,1,0:T(8,128)S(1)} async-done(((f32[32,16,256]{2,1,0:T(8,128)}), f32[32,16,256]{2,1,0:T(8,128)S(1)}, u32[]{:S(2)}, u32[]{:S(2)}) %all-to-all-start) | async-done | bytes 524320 | tf_op jit(solution)/shard_map/all_to_all | solution.py:187
  73.7 0.1 broadcast_multiply_fusion.rows_ref
  73.7 0.0 copy-start
  73.7 0.6 copy-done
  74.3 0.3 convolution_multiply_fusion
  74.6 10.8 %all_to_all.20 = f32[32,4,128]{2,1,0:T(4,128)S(1)} all-to-all(f32[32,4,128]{2,1,0:T(4,128)S(1)} %bitcast.9), channel_id=1, replica_groups=mesh['tgt'=16,'src'=32] {'src'}, dimensions={0} | all-to-all | bytes 131072 | tf_op jit(solution)/shard_map/all_to_all | solution.py:187
  85.4 24.3 %all_to_all.21 = f32[16,4,128]{2,1,0:T(4,128)S(1)} all-to-all(f32[16,4,128]{2,1,0:T(4,128)S(1)} %broadcast_in_dim.7), channel_id=1, replica_groups=mesh['tgt'=16,'src'=32] {'tgt'}, dimensions={0} | all-to-all | bytes 65536 | tf_op jit(solution)/shard_map/all_to_all | solution.py:193
  109.8 12.6 %all_to_all.22 = f32[32,4,128]{2,1,0:T(4,128)} all-to-all(f32[32,4,128]{2,1,0:T(4,128)S(1)} %broadcast_in_dim.8), channel_id=1, replica_groups=mesh['tgt'=16,'src'=32] {'src'}, dimensions={0} | all-to-all | bytes 131072 | tf_op jit(solution)/shard_map/all_to_all | solution.py:193
  122.3 16.2 %shard_map.78 = (f32[128,128]{1,0:T(8,128)}, f32[16,256]{1,0:T(8,128)}) custom-call(f32[128,128]{1,0:T(8,128)} %bitcast.8, f32[16,256]{1,0:T(8,128)} %copy-done), custom_call_target="tpu_custom_call" | custom-call | tf_op jit(solution)/shard_map/pallas_call | solution.py:171
  (6 shorter events, 0.1 us)
Async XLA Ops:
  51.5 22.1 %all-to-all-start = ((f32[32,16,256]{2,1,0:T(8,128)}), f32[32,16,256]{2,1,0:T(8,128)S(1)}, u32[]{:S(2)}, u32[]{:S(2)}) async-start(f32[32,16,256]{2,1,0:T(8,128)} %bitcast.7), calls=%async_computation | async-start | bytes 1048576 | tf_op jit(solution)/shard_map/all_to_all | solution.py:187
  73.7 0.6 copy-start
